TPU v7x, 32 devices: a whole 2x2x4 slice. The times are simulated.
32 devices in a mesh: segment: 2 (over core), expert: 16 (over z, y, x).
Axes of the slice: x: 2, y: 2, z: 4, core: 2. Of those that a mesh axis runs over, the one named last changes fastest.
Arguments:
- hidden_in: bfloat16 [2, 256, 7168], P('segment', 'expert'), may hold values from -6 to 6
- norm_gain: bfloat16 [2, 7168], P('segment'), may hold values from 0.25 to 1.75
- up_proj: bfloat16 [2, 8192, 7168], P('segment', 'expert'), may hold values from -0.0625 to 0.0625
- down_proj: bfloat16 [2, 8192, 7168], P('segment', 'expert'), may hold values from -0.1875 to 0.1875
- expert_ids: int32 [2, 256, 2], P('segment', 'expert'), may hold values from 0 to 7, all different within a row; in each aligned block of 16 rows (0 to 15, 16 to 31, ..., all dimensions but the last counted through in order) at most 7 rows name the same one
- gate_weights: float32 [2, 256, 2], P('segment', 'expert'), may hold values from 0.2 to 1
Outputs:
- handed_on: bfloat16 [2, 256, 7168], P('segment', 'expert')
Inputs may be any that keep to these rules, and one draw needn't show every extreme that they name: `expert_ids`: each row names 2 different experts. Among the rows of one device in one section no expert is named by more than 7 rows, and in some device an expert is named by exactly 7.
All inputs are finite; a program needn't handle non-finite values.
Results may differ from a plain program's by a relative error of at most 0.0075.
Values may be sent and summed in bfloat16 or wider, within the bound.
No kernel may reach another device: no remote copies, remote signals or barrier semaphores. Data moves between devices by JAX's collectives and lax.ppermute only.
A program may use at most 64 MiB of HBM per device.

v0:
```python
import jax
import jax.numpy as jnp
from jax import lax
from jax.sharding import PartitionSpec as P

EXPERTS = 8


def passed_along(shard, axis, by):
    count = lax.axis_size(axis)
    return lax.ppermute(shard, axis, [(i, (i + by) % count) for i in range(count)])


def shards(hidden_in, norm_gain, up_proj, down_proj, expert_ids, gate_weights):
    members = lax.axis_size("expert")
    me = lax.axis_index("expert")
    tokens = hidden_in[0]
    gain = norm_gain[0]
    up_block = up_proj[0]
    down_block = down_proj[0]
    local_units = up_block.shape[0]
    units_per_expert = local_units * members // EXPERTS
    my_expert = me * local_units // units_per_expert
    square = jnp.mean(tokens.astype(jnp.float32) ** 2, axis=-1, keepdims=True)
    normed = (
        tokens.astype(jnp.float32) * lax.rsqrt(square + 1e-06) * gain.astype(jnp.float32)
    ).astype(jnp.bfloat16)
    all_rows = lax.all_gather(normed, "expert", axis=0, tiled=True)
    all_ids = lax.all_gather(expert_ids[0], "expert", axis=0, tiled=True)
    all_gates = lax.all_gather(gate_weights[0], "expert", axis=0, tiled=True)
    scale = jnp.sum(jnp.where(all_ids == my_expert, all_gates, 0.0), axis=-1, keepdims=True)
    inner = jnp.einsum("rd,fd->rf", all_rows, up_block, preferred_element_type=jnp.float32)
    active = jax.nn.silu(inner).astype(jnp.bfloat16)
    partial = jnp.dot(active, down_block, preferred_element_type=jnp.float32).astype(jnp.bfloat16)
    contribution = partial.astype(jnp.float32) * scale
    mixture = lax.psum_scatter(contribution, "expert", scatter_dimension=0, tiled=True)
    section_out = (tokens.astype(jnp.float32) + mixture).astype(jnp.bfloat16)
    handed = passed_along(section_out, "segment", 1)
    return handed[None]


def solution(mesh):
    in_specs = (
        P("segment", "expert", None),
        P("segment", None),
        P("segment", "expert", None),
        P("segment", "expert", None),
        P("segment", "expert", None),
        P("segment", "expert", None),
    )
    out_specs = P("segment", "expert", None)
    return jax.shard_map(shards, mesh=mesh, in_specs=in_specs, out_specs=out_specs, check_vma=False)
```

profile of v0, /device:TPU:11, one launch (start us, length us, event | category | flops | bytes accessed | tf_op | source)
XLA Modules:
  0.0 272.6 jit_solution(9835408425453076009)
XLA Ops:
  6.5 0.0 all-gather.4.cloned.1.call-start
  6.5 1.1 fusion.9
  7.7 0.8 mul.46
  8.4 1.8 fusion.11
  10.2 0.0 all-gather.4.cloned.1.call-update
  10.2 0.0 reduce-scatter.2.cloned.1.call-start
  10.3 0.8 copy.7
  11.0 0.8 copy.8
  11.8 24.2 %all-gather.1 = f32[1,256,2]{2,0,1:T(1,128)S(1)} all-gather(f32[1,16,2]{2,0,1:T(1,128)S(1)} %copy.8), channel_id=3, replica_groups=mesh['segment'=2,'expert'=16] {'expert'}, dimensions={1}, use_global_device_ids=true | all-gather | bytes 2176 | tf_op jit(solution)/shard_map/all_gather | solution.py:30
  36.0 36.2 %all-gather = s32[1,256,2]{2,0,1:T(1,128)S(1)} all-gather(s32[1,16,2]{2,0,1:T(1,128)S(1)} %copy.7), channel_id=2, replica_groups=mesh['segment'=2,'expert'=16] {'expert'}, dimensions={1}, use_global_device_ids=true | all-gather | bytes 2176 | tf_op jit(solution)/shard_map/all_gather | solution.py:29
  72.1 1.0 fusion.14
  73.2 10.5 %all-gather.4.cloned.1.call-done = bf16[256,7168]{1,0:T(8,128)(2,1)} async-done(((bf16[16,7168]{1,0:T(8,128)(2,1)}), bf16[256,7168]{1,0:T(8,128)(2,1)}) %all-gather.4.cloned.1.call-update) | async-done | bytes 3670032 | tf_op jit(solution)/shard_map/all_gather | solution.py:28
  83.7 13.3 %fusion.1 = f32[256,7168]{1,0:T(8,128)} fusion(bf16[1,512,7168]{2,1,0:T(8,128)(2,1)} %param.9, f32[256]{0:T(256)S(1)} %fusion.14, bf16[256,7168]{1,0:T(8,128)(2,1)} %all-gather.4.cloned.1.call-done, bf16[1,512,7168]{2,1,0:T(8,128)(2,1)} %param.8), kind=kOutput, calls=%fused_computation.2 | convolution fusion | flops 3764256768 | bytes 25691136 | tf_op jit(solution)/shard_map/dot_general | solution.py:34
  97.0 0.0 copy-start
  97.0 0.0 reduce-scatter.2.cloned.1.call-update
  97.1 164.8 %reduce-scatter.2.cloned.1.call-done = f32[16,7168]{1,0:T(8,128)} async-done(((f32[256,7168]{1,0:T(8,128)}), f32[16,7168]{1,0:T(8,128)}) %reduce-scatter.2.cloned.1.call-update) | async-done | bytes 458768 | tf_op jit(solution)/shard_map/reduce_scatter | solution.py:36
  261.9 0.0 copy-done
  261.9 1.1 fusion.12
  263.0 1.0 collective-permute-start
  264.0 1.1 collective-permute-done
  265.1 0.7 copy.10
  (1 shorter events, 0.0 us)
Async XLA Ops:
  6.5 77.2 %all-gather.4.cloned.1.call-start = ((), (), s32[]{:S(2)}) async-start(), calls=%async_computation.1 | async-start | bytes 3899392 | tf_op jit(solution)/shard_map/all_gather | solution.py:28
  10.2 251.7 %reduce-scatter.2.cloned.1.call-start = ((), (), s32[]{:S(2)}) async-start(), calls=%async_computation.2 | async-start | bytes 7798784 | tf_op jit(solution)/shard_map/reduce_scatter | solution.py:36
  97.0 164.9 %copy-start = (bf16[1,16,7168]{2,1,0:T(8,128)(2,1)S(1)}, bf16[1,16,7168]{2,1,0:T(8,128)(2,1)}, u32[]{:S(2)}) copy-start(bf16[1,16,7168]{2,1,0:T(8,128)(2,1)} %param.6) | copy-start | bytes 688132
  263.0 2.2 collective-permute-start
Sparse Core Ops, SparseCore 0:
  10.3 73.3 all-gather.3
  97.2 164.6 reduce-scatter.1
where the time goes:
time: 273 us
  waiting for transfers between devices  176 us (64%)
  blocking collectives  60.4 us (22%)
  between operations  13.4 us (5%)
  matrix products  13.3 us (5%)
  other arithmetic  5.74 us (2%)
    reduce_scatter x1, waiting for transfers between devices, shards(): lax.psum_scatter(contribution, 'expert', scatter_dimension=0, tiled=True)  165 us
    all_gather x1, blocking collectives, shards(): all_ids = lax.all_gather(expert_ids[0], 'expert', axis=0, tiled=True)  36.2 us
    all_gather x1, blocking collectives, shards(): all_gates = lax.all_gather(gate_weights[0], 'expert', axis=0, tiled=True)  24.2 us
    dot_general x1, matrix products, shards(): jnp.dot(active, down_block, preferred_element_type=jnp.float32)  13.3 us
    all_gather x1, waiting for transfers between devices, shards(): all_rows = lax.all_gather(normed, 'expert', axis=0, tiled=True)  10.5 us
  transfers between devices with their start and end apart: 3, of which 3 were waited for; matrix products, arithmetic and copies ran while one was open for 1% of the time, Pallas kernels for 0%

commit v1 on v0

--- a/solution.py
+++ b/solution.py
@@ -26,7 +26,24 @@
         tokens.astype(jnp.float32) * lax.rsqrt(square + 1e-06) * gain.astype(jnp.float32)
     ).astype(jnp.bfloat16)
     all_rows = lax.all_gather(normed, "expert", axis=0, tiled=True)
-    all_ids = lax.all_gather(expert_ids[0], "expert", axis=0, tiled=True)
+
+    def advance_seats_all_over_axis(mine, row_axis):
+        count_all = jax.lax.axis_size(row_axis)
+        inbox = [(q, (q + 1) % count_all) for q in range(count_all)]
+
+        def sectors_cover(extra):
+            if len(extra) == count_all:
+                return extra
+            then = sectors_cover(
+                [jax.lax.ppermute(extra[0], axis_name=row_axis, perm=inbox), *extra]
+            )
+            return then
+
+        val2 = jnp.concatenate(sectors_cover([mine]), 0)
+        value_now = jnp.roll(val2, (jax.lax.axis_index(row_axis) + 1) * mine.shape[0], 0)
+        return value_now
+
+    all_ids = advance_seats_all_over_axis(expert_ids[0], "expert")
     all_gates = lax.all_gather(gate_weights[0], "expert", axis=0, tiled=True)
     scale = jnp.sum(jnp.where(all_ids == my_expert, all_gates, 0.0), axis=-1, keepdims=True)
     inner = jnp.einsum("rd,fd->rf", all_rows, up_block, preferred_element_type=jnp.float32)

time: 273 us -> 334 us (1.22)
  waiting for transfers between devices: 176 us -> 272 us
  blocking collectives: 60.4 us -> 24.2 us
    ppermute x0 -> x15, waiting for transfers between devices: none -> 71.3 us  [sectors_cover(): jax.lax.ppermute(extra[0], axis_name=row_axis, perm=inbox)]
    all_gather x1 -> x0, blocking collectives: 36.2 us -> none  [shards(): all_ids = lax.all_gather(expert_ids[0], 'expert', axis=0, tiled=True)]
    reduce_scatter x1, waiting for transfers between devices: 165 us -> 199 us  [shards(): lax.psum_scatter(contribution, 'expert', scatter_dimension=0, tiled=True)]
    all_gather x1, waiting for transfers between devices: 10.5 us -> 0.02 us  [shards(): all_rows = lax.all_gather(normed, 'expert', axis=0, tiled=True)]
  transfers between devices with their start and end apart: 3 -> 18, of which waited for: 3 -> 16; matrix products, arithmetic and copies ran while one was open for 1% -> 1% of each run, Pallas kernels for 0% -> 0%
where the time goes in v1:
time: 334 us; the launch traced here: 333 us
  waiting for transfers between devices  272 us (81%)
  blocking collectives  24.2 us (7%)
  between operations  13.4 us (4%)
  matrix products  13.3 us (4%)
  other arithmetic  4.82 us (1%)
  starting transfers between devices  3.36 us (1%)
    reduce_scatter x1, waiting for transfers between devices, shards(): lax.psum_scatter(contribution, 'expert', scatter_dimension=0, tiled=True)  199 us
    ppermute x15, waiting for transfers between devices, sectors_cover(): jax.lax.ppermute(extra[0], axis_name=row_axis, perm=inbox)  71.3 us
    all_gather x1, blocking collectives, shards(): all_gates = lax.all_gather(gate_weights[0], 'expert', axis=0, tiled=True)  24.2 us
    dot_general x1, matrix products, shards(): jnp.dot(active, down_block, preferred_element_type=jnp.float32)  13.3 us
  transfers between devices with their start and end apart: 18, of which 16 were waited for; matrix products, arithmetic and copies ran while one was open for 1% of the time, Pallas kernels for 0%

profile of v1, /device:TPU:11, one launch (start us, length us, event | category | flops | bytes accessed | tf_op | source)
XLA Modules:
  0.0 333.2 jit_solution(14297542240977863408)
XLA Ops:
  6.5 0.0 all-gather.3.cloned.1.call-start
  6.5 1.1 fusion.9
  7.7 0.8 mul.50
  8.4 1.8 fusion.11
  10.2 0.0 all-gather.3.cloned.1.call-update
  10.2 0.0 reduce-scatter.2.cloned.1.call-start
  10.3 1.3 collective-permute-start
  11.5 0.8 copy.7
  12.3 24.2 %all-gather = f32[1,256,2]{2,0,1:T(1,128)S(1)} all-gather(f32[1,16,2]{2,0,1:T(1,128)S(1)} %copy.7), channel_id=2, replica_groups=mesh['segment'=2,'expert'=16] {'expert'}, dimensions={1}, use_global_device_ids=true | all-gather | bytes 2176 | tf_op jit(solution)/shard_map/all_gather | solution.py:47
  36.5 0.0 collective-permute-done
  36.5 1.0 collective-permute-start.1
  37.5 4.1 %collective-permute-done.1 = s32[16,2]{0,1:T(2,128)S(1)} collective-permute-done((s32[16,2]{0,1:T(2,128)S(1)}, s32[16,2]{0,1:T(2,128)S(1)}, u32[]{:S(2)}, u32[]{:S(2)}) %collective-permute-start.1) | collective-permute-done | bytes 160 | tf_op jit(solution)/shard_map/ppermute | solution.py:38
  41.6 0.0 collective-permute-start.2
  41.6 4.2 %collective-permute-done.2 = s32[16,2]{0,1:T(2,128)S(1)} collective-permute-done((s32[16,2]{0,1:T(2,128)S(1)}, s32[16,2]{0,1:T(2,128)S(1)}, u32[]{:S(2)}, u32[]{:S(2)}) %collective-permute-start.2) | collective-permute-done | bytes 160 | tf_op jit(solution)/shard_map/ppermute | solution.py:38
  45.8 0.0 collective-permute-start.3
  45.8 4.0 %collective-permute-done.3 = s32[16,2]{0,1:T(2,128)S(1)} collective-permute-done((s32[16,2]{0,1:T(2,128)S(1)}, s32[16,2]{0,1:T(2,128)S(1)}, u32[]{:S(2)}, u32[]{:S(2)}) %collective-permute-start.3) | collective-permute-done | bytes 160 | tf_op jit(solution)/shard_map/ppermute | solution.py:38
  49.8 0.0 collective-permute-start.4
  49.8 4.1 %collective-permute-done.4 = s32[16,2]{0,1:T(2,128)S(1)} collective-permute-done((s32[16,2]{0,1:T(2,128)S(1)}, s32[16,2]{0,1:T(2,128)S(1)}, u32[]{:S(2)}, u32[]{:S(2)}) %collective-permute-start.4) | collective-permute-done | bytes 160 | tf_op jit(solution)/shard_map/ppermute | solution.py:38
  53.9 0.0 collective-permute-start.5
  53.9 4.2 %collective-permute-done.5 = s32[16,2]{0,1:T(2,128)S(1)} collective-permute-done((s32[16,2]{0,1:T(2,128)S(1)}, s32[16,2]{0,1:T(2,128)S(1)}, u32[]{:S(2)}, u32[]{:S(2)}) %collective-permute-start.5) | collective-permute-done | bytes 160 | tf_op jit(solution)/shard_map/ppermute | solution.py:38
  58.1 0.0 collective-permute-start.6
  58.1 4.6 %collective-permute-done.6 = s32[16,2]{0,1:T(2,128)S(1)} collective-permute-done((s32[16,2]{0,1:T(2,128)S(1)}, s32[16,2]{0,1:T(2,128)S(1)}, u32[]{:S(2)}, u32[]{:S(2)}) %collective-permute-start.6) | collective-permute-done | bytes 160 | tf_op jit(solution)/shard_map/ppermute | solution.py:38
  62.7 0.0 collective-permute-start.7
  62.7 4.8 %collective-permute-done.7 = s32[16,2]{0,1:T(2,128)S(1)} collective-permute-done((s32[16,2]{0,1:T(2,128)S(1)}, s32[16,2]{0,1:T(2,128)S(1)}, u32[]{:S(2)}, u32[]{:S(2)}) %collective-permute-start.7) | collective-permute-done | bytes 160 | tf_op jit(solution)/shard_map/ppermute | solution.py:38
  67.6 0.0 collective-permute-start.8
  67.6 6.4 %collective-permute-done.8 = s32[16,2]{0,1:T(2,128)S(1)} collective-permute-done((s32[16,2]{0,1:T(2,128)S(1)}, s32[16,2]{0,1:T(2,128)S(1)}, u32[]{:S(2)}, u32[]{:S(2)}) %collective-permute-start.8) | collective-permute-done | bytes 160 | tf_op jit(solution)/shard_map/ppermute | solution.py:38
  74.0 0.0 collective-permute-start.9
  74.0 5.8 %collective-permute-done.9 = s32[16,2]{0,1:T(2,128)S(1)} collective-permute-done((s32[16,2]{0,1:T(2,128)S(1)}, s32[16,2]{0,1:T(2,128)S(1)}, u32[]{:S(2)}, u32[]{:S(2)}) %collective-permute-start.9) | collective-permute-done | bytes 160 | tf_op jit(solution)/shard_map/ppermute | solution.py:38
  79.8 0.0 collective-permute-start.10
  79.8 6.2 %collective-permute-done.10 = s32[16,2]{0,1:T(2,128)S(1)} collective-permute-done((s32[16,2]{0,1:T(2,128)S(1)}, s32[16,2]{0,1:T(2,128)S(1)}, u32[]{:S(2)}, u32[]{:S(2)}) %collective-permute-start.10) | collective-permute-done | bytes 160 | tf_op jit(solution)/shard_map/ppermute | solution.py:38
  86.0 0.0 collective-permute-start.11
  86.0 5.1 %collective-permute-done.11 = s32[16,2]{0,1:T(2,128)S(1)} collective-permute-done((s32[16,2]{0,1:T(2,128)S(1)}, s32[16,2]{0,1:T(2,128)S(1)}, u32[]{:S(2)}, u32[]{:S(2)}) %collective-permute-start.11) | collective-permute-done | bytes 160 | tf_op jit(solution)/shard_map/ppermute | solution.py:38
  91.1 0.0 collective-permute-start.12
  91.1 0.1 copy.8
  91.2 5.7 %collective-permute-done.12 = s32[16,2]{0,1:T(2,128)S(1)} collective-permute-done((s32[16,2]{0,1:T(2,128)S(1)}, s32[16,2]{0,1:T(2,128)S(1)}, u32[]{:S(2)}, u32[]{:S(2)}) %collective-permute-start.12) | collective-permute-done | bytes 160 | tf_op jit(solution)/shard_map/ppermute | solution.py:38
  96.9 0.0 collective-permute-start.13
  96.9 6.0 %collective-permute-done.13 = s32[16,2]{0,1:T(2,128)S(1)} collective-permute-done((s32[16,2]{0,1:T(2,128)S(1)}, s32[16,2]{0,1:T(2,128)S(1)}, u32[]{:S(2)}, u32[]{:S(2)}) %collective-permute-start.13) | collective-permute-done | bytes 160 | tf_op jit(solution)/shard_map/ppermute | solution.py:38
  102.9 0.0 collective-permute-start.14
  102.9 6.0 %collective-permute-done.14 = s32[16,2]{0,1:T(2,128)S(1)} collective-permute-done((s32[16,2]{0,1:T(2,128)S(1)}, s32[16,2]{0,1:T(2,128)S(1)}, u32[]{:S(2)}, u32[]{:S(2)}) %collective-permute-start.14) | collective-permute-done | bytes 160 | tf_op jit(solution)/shard_map/ppermute | solution.py:38
  108.9 0.9 concatenate.6
  109.8 0.1 fusion.14
  109.9 0.0 all-gather.3.cloned.1.call-done
  109.9 13.3 %fusion.1 = f32[256,7168]{1,0:T(8,128)} fusion(bf16[1,512,7168]{2,1,0:T(8,128)(2,1)} %param.9, f32[256]{0:T(256)S(1)} %fusion.14, bf16[256,7168]{1,0:T(8,128)(2,1)} %all-gather.3.cloned.1.call-done, bf16[1,512,7168]{2,1,0:T(8,128)(2,1)} %param.8), kind=kOutput, calls=%fused_computation.2 | convolution fusion | flops 3764256768 | bytes 25691136 | tf_op jit(solution)/shard_map/dot_general | solution.py:51
  123.2 0.0 copy-start
  123.2 0.0 reduce-scatter.2.cloned.1.call-update
  123.2 199.2 %reduce-scatter.2.cloned.1.call-done = f32[16,7168]{1,0:T(8,128)} async-done(((f32[256,7168]{1,0:T(8,128)}), f32[16,7168]{1,0:T(8,128)}) %reduce-scatter.2.cloned.1.call-update) | async-done | bytes 458768 | tf_op jit(solution)/shard_map/reduce_scatter | solution.py:53
  322.5 0.0 copy-done
  322.5 1.1 fusion.12
  323.5 1.1 collective-permute-start.15
  324.6 1.1 collective-permute-done.15
  325.7 0.7 copy.10
  (1 shorter events, 0.0 us)
Async XLA Ops:
  6.5 103.3 %all-gather.3.cloned.1.call-start = ((), (), s32[]{:S(2)}) async-start(), calls=%async_computation.1 | async-start | bytes 3899392 | tf_op jit(solution)/shard_map/all_gather | solution.py:28
  10.2 312.2 %reduce-scatter.2.cloned.1.call-start = ((), (), s32[]{:S(2)}) async-start(), calls=%async_computation.2 | async-start | bytes 7798784 | tf_op jit(solution)/shard_map/reduce_scatter | solution.py:53
  10.3 26.2 %collective-permute-start = (s32[16,2]{0,1:T(2,128)}, s32[16,2]{0,1:T(2,128)S(1)}, u32[]{:S(2)}, u32[]{:S(2)}) collective-permute-start(s32[16,2]{0,1:T(2,128)} %bitcast.23), channel_id=1, source_target_pairs={{0,1},{1,2},{2,3},{3,4},{4,5},{5,6},{6,7},{7,8},{8,9},{9,10},{10,1... | collective-permute-start | bytes 392 | tf_op jit(solution)/shard_map/ppermute | solution.py:38
  36.5 5.1 %collective-permute-start.1 = (s32[16,2]{0,1:T(2,128)S(1)}, s32[16,2]{0,1:T(2,128)S(1)}, u32[]{:S(2)}, u32[]{:S(2)}) collective-permute-start(s32[16,2]{0,1:T(2,128)S(1)} %collective-permute-done), channel_id=1, source_target_pairs={{0,1},{1,2},{2,3},{3,4},{4,5},{5,6},{6,7},{7,8},{8,9},{9,10},{10,1... | collective-permute-start | bytes 392 | tf_op jit(solution)/shard_map/ppermute | solution.py:38
  41.6 4.2 %collective-permute-start.2 = (s32[16,2]{0,1:T(2,128)S(1)}, s32[16,2]{0,1:T(2,128)S(1)}, u32[]{:S(2)}, u32[]{:S(2)}) collective-permute-start(s32[16,2]{0,1:T(2,128)S(1)} %collective-permute-done.1), channel_id=1, source_target_pairs={{0,1},{1,2},{2,3},{3,4},{4,5},{5,6},{6,7},{7,8},{8,9},{9,10},{10,1... | collective-permute-start | bytes 392 | tf_op jit(solution)/shard_map/ppermute | solution.py:38
  45.8 4.0 %collective-permute-start.3 = (s32[16,2]{0,1:T(2,128)S(1)}, s32[16,2]{0,1:T(2,128)S(1)}, u32[]{:S(2)}, u32[]{:S(2)}) collective-permute-start(s32[16,2]{0,1:T(2,128)S(1)} %collective-permute-done.2), channel_id=1, source_target_pairs={{0,1},{1,2},{2,3},{3,4},{4,5},{5,6},{6,7},{7,8},{8,9},{9,10},{10,1... | collective-permute-start | bytes 392 | tf_op jit(solution)/shard_map/ppermute | solution.py:38
  49.8 4.1 %collective-permute-start.4 = (s32[16,2]{0,1:T(2,128)S(1)}, s32[16,2]{0,1:T(2,128)S(1)}, u32[]{:S(2)}, u32[]{:S(2)}) collective-permute-start(s32[16,2]{0,1:T(2,128)S(1)} %collective-permute-done.3), channel_id=1, source_target_pairs={{0,1},{1,2},{2,3},{3,4},{4,5},{5,6},{6,7},{7,8},{8,9},{9,10},{10,1... | collective-permute-start | bytes 392 | tf_op jit(solution)/shard_map/ppermute | solution.py:38
  53.9 4.2 %collective-permute-start.5 = (s32[16,2]{0,1:T(2,128)S(1)}, s32[16,2]{0,1:T(2,128)S(1)}, u32[]{:S(2)}, u32[]{:S(2)}) collective-permute-start(s32[16,2]{0,1:T(2,128)S(1)} %collective-permute-done.4), channel_id=1, source_target_pairs={{0,1},{1,2},{2,3},{3,4},{4,5},{5,6},{6,7},{7,8},{8,9},{9,10},{10,1... | collective-permute-start | bytes 392 | tf_op jit(solution)/shard_map/ppermute | solution.py:38
  58.1 4.6 %collective-permute-start.6 = (s32[16,2]{0,1:T(2,128)S(1)}, s32[16,2]{0,1:T(2,128)S(1)}, u32[]{:S(2)}, u32[]{:S(2)}) collective-permute-start(s32[16,2]{0,1:T(2,128)S(1)} %collective-permute-done.5), channel_id=1, source_target_pairs={{0,1},{1,2},{2,3},{3,4},{4,5},{5,6},{6,7},{7,8},{8,9},{9,10},{10,1... | collective-permute-start | bytes 392 | tf_op jit(solution)/shard_map/ppermute | solution.py:38
  62.7 4.8 %collective-permute-start.7 = (s32[16,2]{0,1:T(2,128)S(1)}, s32[16,2]{0,1:T(2,128)S(1)}, u32[]{:S(2)}, u32[]{:S(2)}) collective-permute-start(s32[16,2]{0,1:T(2,128)S(1)} %collective-permute-done.6), channel_id=1, source_target_pairs={{0,1},{1,2},{2,3},{3,4},{4,5},{5,6},{6,7},{7,8},{8,9},{9,10},{10,1... | collective-permute-start | bytes 392 | tf_op jit(solution)/shard_map/ppermute | solution.py:38
  67.6 6.4 %collective-permute-start.8 = (s32[16,2]{0,1:T(2,128)S(1)}, s32[16,2]{0,1:T(2,128)S(1)}, u32[]{:S(2)}, u32[]{:S(2)}) collective-permute-start(s32[16,2]{0,1:T(2,128)S(1)} %collective-permute-done.7), channel_id=1, source_target_pairs={{0,1},{1,2},{2,3},{3,4},{4,5},{5,6},{6,7},{7,8},{8,9},{9,10},{10,1... | collective-permute-start | bytes 392 | tf_op jit(solution)/shard_map/ppermute | solution.py:38
  74.0 5.8 %collective-permute-start.9 = (s32[16,2]{0,1:T(2,128)S(1)}, s32[16,2]{0,1:T(2,128)S(1)}, u32[]{:S(2)}, u32[]{:S(2)}) collective-permute-start(s32[16,2]{0,1:T(2,128)S(1)} %collective-permute-done.8), channel_id=1, source_target_pairs={{0,1},{1,2},{2,3},{3,4},{4,5},{5,6},{6,7},{7,8},{8,9},{9,10},{10,1... | collective-permute-start | bytes 392 | tf_op jit(solution)/shard_map/ppermute | solution.py:38
  79.8 6.2 %collective-permute-start.10 = (s32[16,2]{0,1:T(2,128)S(1)}, s32[16,2]{0,1:T(2,128)S(1)}, u32[]{:S(2)}, u32[]{:S(2)}) collective-permute-start(s32[16,2]{0,1:T(2,128)S(1)} %collective-permute-done.9), channel_id=1, source_target_pairs={{0,1},{1,2},{2,3},{3,4},{4,5},{5,6},{6,7},{7,8},{8,9},{9,10},{10,1... | collective-permute-start | bytes 392 | tf_op jit(solution)/shard_map/ppermute | solution.py:38
  86.0 5.1 %collective-permute-start.11 = (s32[16,2]{0,1:T(2,128)S(1)}, s32[16,2]{0,1:T(2,128)S(1)}, u32[]{:S(2)}, u32[]{:S(2)}) collective-permute-start(s32[16,2]{0,1:T(2,128)S(1)} %collective-permute-done.10), channel_id=1, source_target_pairs={{0,1},{1,2},{2,3},{3,4},{4,5},{5,6},{6,7},{7,8},{8,9},{9,10},{10,1... | collective-permute-start | bytes 392 | tf_op jit(solution)/shard_map/ppermute | solution.py:38
  91.1 5.8 %collective-permute-start.12 = (s32[16,2]{0,1:T(2,128)S(1)}, s32[16,2]{0,1:T(2,128)S(1)}, u32[]{:S(2)}, u32[]{:S(2)}) collective-permute-start(s32[16,2]{0,1:T(2,128)S(1)} %collective-permute-done.11), channel_id=1, source_target_pairs={{0,1},{1,2},{2,3},{3,4},{4,5},{5,6},{6,7},{7,8},{8,9},{9,10},{10,1... | collective-permute-start | bytes 392 | tf_op jit(solution)/shard_map/ppermute | solution.py:38
  96.9 6.0 %collective-permute-start.13 = (s32[16,2]{0,1:T(2,128)S(1)}, s32[16,2]{0,1:T(2,128)S(1)}, u32[]{:S(2)}, u32[]{:S(2)}) collective-permute-start(s32[16,2]{0,1:T(2,128)S(1)} %collective-permute-done.12), channel_id=1, source_target_pairs={{0,1},{1,2},{2,3},{3,4},{4,5},{5,6},{6,7},{7,8},{8,9},{9,10},{10,1... | collective-permute-start | bytes 392 | tf_op jit(solution)/shard_map/ppermute | solution.py:38
  102.9 6.0 %collective-permute-start.14 = (s32[16,2]{0,1:T(2,128)S(1)}, s32[16,2]{0,1:T(2,128)S(1)}, u32[]{:S(2)}, u32[]{:S(2)}) collective-permute-start(s32[16,2]{0,1:T(2,128)S(1)} %collective-permute-done.13), channel_id=1, source_target_pairs={{0,1},{1,2},{2,3},{3,4},{4,5},{5,6},{6,7},{7,8},{8,9},{9,10},{10,1... | collective-permute-start | bytes 392 | tf_op jit(solution)/shard_map/ppermute | solution.py:38
  123.2 199.2 %copy-start = (bf16[1,16,7168]{2,1,0:T(8,128)(2,1)S(1)}, bf16[1,16,7168]{2,1,0:T(8,128)(2,1)}, u32[]{:S(2)}) copy-start(bf16[1,16,7168]{2,1,0:T(8,128)(2,1)} %param.6) | copy-start | bytes 688132
  323.5 2.2 collective-permute-start.15
Sparse Core Ops, SparseCore 0:
  10.3 72.1 all-gather.2
  123.4 199.0 reduce-scatter.1
